TPU v7x, 32 devices: a whole 2x2x4 slice. The times are simulated.
32 devices in a mesh: groups: 2 (over y), inner: 16 (over z, x, core).
Axes of the slice: x: 2, y: 2, z: 4, core: 2. Of those that a mesh axis runs over, the one named last changes fastest.
Arguments:
- ticks: bfloat16 [262144, 128], P(('groups', 'inner')), parts along dimension 0, may hold values from -6 to 6
- conv_weight: bfloat16 [2048, 768], replicated, may hold values from -0.125 to 0.125
- norm_gain: float32 [768], replicated, may hold values from 0.25 to 1.75
- qkv_weight: bfloat16 [768, 2304], replicated, may hold values from -0.21875 to 0.21875
- head_gain: float32 [768], replicated, may hold values from 0.25 to 1.75
- out_weight: bfloat16 [768, 768], replicated, may hold values from -0.21875 to 0.21875
- state_in: float32 [24, 64, 64], P('groups'), parts along dimension 0, may hold values from -768 to 768
Outputs:
- layer_out: bfloat16 [32768, 768], P(('groups', 'inner')), parts along dimension 0
There are 2 independent parts, one for each index of `groups`. A program takes and returns all parts, laid end to end along the dimension named above; an argument that names none is the same for every part. Nothing has to cross between parts.
All inputs are finite; a program needn't handle non-finite values.
Results may differ from a plain program's by a relative error of at most 0.008.
Values may be sent and summed in bfloat16 or wider, within the bound.
No kernel may reach another device: no remote copies, remote signals or barrier semaphores. Data moves between devices by JAX's collectives and lax.ppermute only.
A program may use at most 192 MiB of HBM per device.

v0:
```python
import jax
import jax.numpy as jnp
from jax import lax
from jax.sharding import PartitionSpec as P

STRIDE = 8
BLK = 512


def from_behind(value, axis, steps):
    count = lax.axis_size(axis)
    initial, last = (max(0, -steps), min(count, count - steps))
    return lax.ppermute(value, axis, [(source, source + steps) for source in range(initial, last)])


def shards(ticks, conv_weight, norm_gain, qkv_weight, head_gain, out_weight, state_in):
    row_width = STRIDE * ticks.shape[1]
    token_count = ticks.shape[0] // STRIDE
    tick_rows = ticks.reshape(token_count, row_width)
    weight_prev = conv_weight[:row_width]
    current = jnp.dot(tick_rows, conv_weight[row_width:], preferred_element_type=jnp.float32)
    last_row = from_behind(tick_rows[token_count - 1 :], "inner", 1)
    earlier_rows = jnp.concatenate([last_row, tick_rows[:-1]], 0)
    embedded_f = current + jnp.dot(earlier_rows, weight_prev, preferred_element_type=jnp.float32)
    embedded = embedded_f.astype(jnp.bfloat16)
    embed_f = embedded.astype(jnp.float32)
    normed = (
        embed_f * lax.rsqrt(jnp.mean(embed_f * embed_f, -1, keepdims=True) + 1e-05) * norm_gain
    ).astype(jnp.bfloat16)
    qkv = jnp.dot(normed, qkv_weight, preferred_element_type=jnp.float32).astype(jnp.bfloat16)
    model_width = embedded.shape[1]
    head_count = state_in.shape[0]
    head_size = state_in.shape[1]
    block_count = token_count // BLK
    queries = qkv[:, :model_width].reshape(block_count, BLK, head_count, head_size)
    keys_all = qkv[:, model_width : 2 * model_width].reshape(
        block_count, BLK, head_count, head_size
    )
    values_all = qkv[:, 2 * model_width :].reshape(block_count, BLK, head_count, head_size)
    block_states = jnp.einsum(
        "bthi,bthj->bhij", keys_all, values_all, preferred_element_type=jnp.float32
    )
    local_state = jnp.sum(block_states, 0)
    every_state = lax.all_gather(local_state[None], "inner", axis=0, tiled=True)
    lower_dev = (jnp.arange(every_state.shape[0]) < lax.axis_index("inner")).astype(jnp.float32)
    prefix = jnp.einsum("n,nhij->hij", lower_dev, every_state, precision=lax.Precision.HIGHEST)
    carried = state_in + prefix
    within = jnp.cumsum(block_states, 0) - block_states
    state_before = carried[None] + within
    lower = jnp.arange(BLK)[:, None] >= jnp.arange(BLK)[None, :]
    scores = jnp.einsum("bthd,bshd->bhts", queries, keys_all, preferred_element_type=jnp.float32)
    scores = jnp.where(lower[None, None], scores, 0.0).astype(jnp.bfloat16)
    inside_term = jnp.einsum(
        "bhts,bshd->bthd", scores, values_all, preferred_element_type=jnp.float32
    )
    carried_term = jnp.einsum(
        "bthi,bhij->bthj",
        queries.astype(jnp.float32),
        state_before,
        precision=lax.Precision.HIGHEST,
    )
    combined = (inside_term + carried_term).reshape(token_count, head_count, head_size)
    attended = (
        combined
        * lax.rsqrt(jnp.mean(combined * combined, -1, keepdims=True) + 1e-06)
        * head_gain.reshape(head_count, head_size)
    )
    attended = attended.reshape(token_count, model_width).astype(jnp.bfloat16)
    return (embed_f + jnp.dot(attended, out_weight, preferred_element_type=jnp.float32)).astype(
        jnp.bfloat16
    )


def solution(mesh):
    in_specs = (P(("groups", "inner"), None), P(), P(), P(), P(), P(), P("groups", None, None))
    out_specs = P(("groups", "inner"), None)
    return jax.shard_map(shards, mesh=mesh, in_specs=in_specs, out_specs=out_specs, check_vma=False)
```

profile of v0, /device:TPU:0, one launch (start us, length us, event | category | flops | bytes accessed | tf_op | source)
XLA Modules:
  0.0 145.3 jit_solution(13970756868127508273)
XLA Ops:
  6.5 0.8 slice_bitcast_fusion
  7.4 2.5 %collective-permute-start = (bf16[1,1024]{1,0:T(2,128)(2,1)S(1)}, bf16[1,1024]{1,0:T(2,128)(2,1)S(1)}, u32[]{:S(2)}, u32[]{:S(2)}) collective-permute-start(bf16[1,1024]{1,0:T(2,128)(2,1)S(1)} %bitcast.53), channel_id=1, source_target_pairs={{0,1},{1,2},{2,3},{3,4},{4,5},{5,6},{6,7},{7,8},{8,9},{9,10},{10,1... | collective-permute-start | bytes 6152 | tf_op jit(solution)/shard_map/ppermute | solution.py:13
  9.9 4.2 %reshape.62 = bf16[1024,1024]{1,0:T(8,128)(2,1)} reshape(bf16[8192,128]{1,0:T(8,128)(2,1)} %param.7) | data formatting | bytes 4194304 | tf_op jit(solution)/shard_map/reshape | solution.py:19
  14.0 5.7 %fusion.21 = f32[1024,768]{0,1:T(8,128)} fusion(bf16[1024,1024]{1,0:T(8,128)(2,1)} %reshape.62, bf16[2048,768]{1,0:T(8,128)(2,1)} %param.8), kind=kOutput, calls=%fused_computation.28 | convolution fusion | flops 1610612736 | bytes 6815744 | tf_op jit(solution)/shard_map/dot_general | solution.py:21
  19.7 1.5 %slice.30 = bf16[8184,128]{1,0:T(8,128)(2,1)} slice(bf16[8192,128]{1,0:T(8,128)(2,1)S(1)} %copy-done.2), slice={[0:8184], [0:128]} | slice | bytes 4190208 | tf_op jit(solution)/shard_map/slice | solution.py:23
  21.2 4.2 %slice.31 = bf16[1023,1024]{1,0:T(8,128)(2,1)} reshape(bf16[8184,128]{1,0:T(8,128)(2,1)} %slice.30) | data formatting | bytes 4190208 | tf_op jit(solution)/shard_map/slice | solution.py:23
  25.3 5.0 %fusion.7 = (f32[1024]{0:T(1024)S(1)}, bf16[1024,768]{0,1:T(8,128)(2,1)S(1)}) fusion(f32[1024,768]{0,1:T(8,128)} %fusion.21, bf16[2048,768]{1,0:T(8,128)(2,1)} %param.8, bf16[1023,1024]{1,0:T(8,128)(2,1)} %slice.31, bf16[1,1024]{1,0:T(2,128)(2,1)S(1)} %collective-permute-done), kind=kOutput, calls=%fused_computation.11 | convolution fusion | flops 1618738176 | bytes 8394752 | tf_op jit(solution)/shard_map/dot_general | solution.py:24
  30.4 4.4 %convolution_convert_fusion = bf16[1024,2304]{1,0:T(8,128)(2,1)S(1)} fusion(bf16[768,2304]{1,0:T(8,128)(2,1)S(1)} %copy-done, bf16[1024,768]{0,1:T(8,128)(2,1)S(1)} %get-tuple-element.9, f32[768]{0:T(1024)S(1)} %copy-done.11, f32[1024]{0:T(1024)S(1)} %add_rsqrt_fusion.1), kind=kOutput, calls=%fused_computation.7 | convolution fusion | flops 3629383680 | bytes 9837568 | tf_op jit(solution)/shard_map/dot_general | solution.py:30
  34.8 1.5 %fusion.43 = (bf16[1024,768]{1,0:T(8,128)(2,1)S(1)}, bf16[1024,768]{1,0:T(8,128)(2,1)S(1)}, bf16[1024,768]{1,0:T(8,128)(2,1)}) fusion(bf16[1024,2304]{1,0:T(8,128)(2,1)S(1)} %convolution_convert_fusion), kind=kLoop, calls=%fused_computation.51 | loop fusion | bytes 9437184 | tf_op jit(solution)/shard_map/slice | solution.py:35
  36.2 2.6 %copy.39 = bf16[1024,768]{0,1:T(8,128)(2,1)} copy(bf16[1024,768]{1,0:T(8,128)(2,1)} %get-tuple-element.7) | data formatting | bytes 3145728 | tf_op jit(solution)/shard_map/slice | solution.py:39
  38.8 3.9 %reshape.63 = bf16[2,512,12,64]{1,0,3,2:T(2,128)(2,1)} reshape(bf16[1024,768]{0,1:T(8,128)(2,1)} %copy.39) | data formatting | bytes 3145728 | tf_op jit(solution)/shard_map/reshape | solution.py:39
  42.7 1.7 %copy.41 = bf16[1024,768]{0,1:T(8,128)(2,1)} copy(bf16[1024,768]{1,0:T(8,128)(2,1)S(1)} %get-tuple-element.6) | data formatting | bytes 3145728 | tf_op jit(solution)/shard_map/slice | solution.py:36
  44.4 4.0 %reshape.65 = bf16[2,512,12,64]{1,0,3,2:T(2,128)(2,1)} reshape(bf16[1024,768]{0,1:T(8,128)(2,1)} %copy.41) | data formatting | bytes 3145728 | tf_op jit(solution)/shard_map/reshape | solution.py:36
  48.3 3.7 %fusion.44 = (f32[12,64,64]{2,1,0:T(8,128)}, f32[2,12,64,64]{3,2,1,0:T(8,128)}) fusion(bf16[2,512,12,64]{1,0,3,2:T(2,128)(2,1)S(1)} %copy-done.7, bf16[2,512,12,64]{1,0,3,2:T(2,128)(2,1)} %reshape.65), kind=kOutput, calls=%fused_computation.52 | convolution fusion | flops 100712448 | bytes 3735552 | tf_op jit(solution)/shard_map/bthi,bthj->bhij/dot_general | solution.py:40
  52.0 0.0 all-gather.3.cloned.1.call-update
  52.0 0.1 iota_compare_fusion
  52.1 0.8 copy.40
  52.9 1.2 reshape.64
  54.1 10.5 %fusion = f32[2,12,64,512]{3,2,1,0:T(8,128)} fusion(pred[512,512]{1,0:T(8,128)(4,1)S(1)} %iota_compare_fusion, bf16[2,512,12,64]{1,0,3,2:T(2,128)(2,1)} %reshape.63, bf16[2,512,12,64]{1,0,3,2:T(2,128)(2,1)} %reshape.65, bf16[2,512,12,64]{1,0,3,2:T(2,128)(2,1)S(1)} %reshape.64), kind=kOutput, calls=%fused_computation.1 | convolution fusion | flops 1623195648 | bytes 8126464 | tf_op jit(solution)/shard_map/bhts,bshd->bthd/dot_general | solution.py:53
  64.6 52.0 %all-gather.3.cloned.1.call-done = f32[192,64,64]{2,1,0:T(8,128)} async-done(((f32[12,64,64]{2,1,0:T(8,128)}), f32[192,64,64]{2,1,0:T(8,128)}) %all-gather.3.cloned.1.call-update) | async-done | bytes 3145744 | tf_op jit(solution)/shard_map/all_gather | solution.py:44
  116.6 8.4 %fusion.5 = f32[1,12,64,64]{3,0,2,1:T(1,128)S(1)} fusion(f32[16,12,64,64]{3,2,1,0:T(8,128)} %bitcast.48, s32[]{:T(128)S(6)} %axis_index.12), kind=kOutput, calls=%fused_computation.5 | convolution fusion | flops 9437200 | bytes 3342340 | tf_op jit(solution)/shard_map/n,nhij->hij/dot_general | solution.py:46
  125.1 0.5 fusion.27
  125.6 0.8 copy-done.4
  126.4 1.7 %multiply_reduce_fusion = (f32[2,512,12]{1,2,0:T(8,128)S(1)}, f32[2,512,12,64]{1,3,2,0:T(8,128)S(1)}) fusion(f32[2,12,64,512]{3,2,1,0:T(8,128)S(1)} %copy-done.5, f32[2,12,64,64]{3,2,1,0:T(8,128)S(1)} %fusion.27, bf16[2,512,12,64]{1,0,3,2:T(2,128)(2,1)S(1)} %copy-done.4), kind=kOutput, calls=%fused_computation.18 | convolution fusion | flops 606326784 | bytes 8306688 | tf_op jit(solution)/shard_map/bthi,bhij->bthj/dot_general | solution.py:56
  128.2 2.4 %copy.49 = f32[2,512,12,64]{1,0,3,2:T(2,128)S(1)} copy(f32[2,512,12,64]{1,3,2,0:T(8,128)S(1)} %get-tuple-element.13) | data formatting | bytes 6291456 | tf_op jit(solution)/shard_map/add | solution.py:62
  130.6 0.7 copy.59
  131.5 0.0 copy-start.10
  131.5 0.4 fusion.12
  131.9 0.9 copy-done.10
  132.8 0.5 copy-done.13
  133.3 2.6 %fusion.10 = bf16[1024,768]{0,1:T(8,128)(2,1)} fusion(bf16[1024,768]{0,1:T(8,128)(2,1)S(1)} %copy-done.13, bf16[1024,768]{0,1:T(8,128)(2,1)S(1)} %fusion.12, bf16[768,768]{1,0:T(8,128)(2,1)S(1)} %copy-done.10), kind=kOutput, calls=%fused_computation.14 | convolution fusion | flops 1210318848 | bytes 5898240 | tf_op jit(solution)/shard_map/dot_general | solution.py:69
  135.9 2.6 %copy.52 = bf16[1024,768]{1,0:T(8,128)(2,1)} copy(bf16[1024,768]{0,1:T(8,128)(2,1)} %fusion.10) | data formatting | bytes 3145728 | tf_op jit(solution)/shard_map/convert_element_type | solution.py:69
  (33 shorter events, 0.2 us)
Async XLA Ops:
  6.5 23.8 %copy-start = (bf16[768,2304]{1,0:T(8,128)(2,1)S(1)}, bf16[768,2304]{1,0:T(8,128)(2,1)}, u32[]{:S(2)}) copy-start(bf16[768,2304]{1,0:T(8,128)(2,1)} %param.10) | copy-start | bytes 10616836
  6.5 110.0 %all-gather.3.cloned.1.call-start = ((), (), s32[]{:S(2)}) async-start(), calls=%async_computation | async-start | bytes 6684672 | tf_op jit(solution)/shard_map/all_gather | solution.py:44
  7.4 18.0 %collective-permute-start = (bf16[1,1024]{1,0:T(2,128)(2,1)S(1)}, bf16[1,1024]{1,0:T(2,128)(2,1)S(1)}, u32[]{:S(2)}, u32[]{:S(2)}) collective-permute-start(bf16[1,1024]{1,0:T(2,128)(2,1)S(1)} %bitcast.53), channel_id=1, source_target_pairs={{0,1},{1,2},{2,3},{3,4},{4,5},{5,6},{6,7},{7,8},{8,9},{9,10},{10,1... | collective-permute-start | bytes 6152 | tf_op jit(solution)/shard_map/ppermute | solution.py:13
  14.0 5.7 %copy-start.2 = (bf16[8192,128]{1,0:T(8,128)(2,1)S(1)}, bf16[8192,128]{1,0:T(8,128)(2,1)}, u32[]{:S(2)}) copy-start(bf16[8192,128]{1,0:T(8,128)(2,1)} %param.7) | copy-start | bytes 6291460
  25.3 5.0 %copy-start.11 = (f32[768]{0:T(1024)S(1)}, f32[768]{0:T(1024)}, u32[]{:S(2)}) copy-start(f32[768]{0:T(1024)} %param.9) | copy-start | bytes 9220
  30.3 4.4 %copy-start.12 = (bf16[1024,768]{0,1:T(8,128)(2,1)}, bf16[1024,768]{0,1:T(8,128)(2,1)S(1)}, u32[]{:S(2)}) copy-start(bf16[1024,768]{0,1:T(8,128)(2,1)S(1)} %get-tuple-element.9) | copy-start | bytes 4718596
  44.4 4.0 %copy-start.7 = (bf16[2,512,12,64]{1,0,3,2:T(2,128)(2,1)S(1)}, bf16[2,512,12,64]{1,0,3,2:T(2,128)(2,1)}, u32[]{:S(2)}) copy-start(bf16[2,512,12,64]{1,0,3,2:T(2,128)(2,1)} %reshape.63) | copy-start | bytes 4718596
  54.1 10.5 %copy-start.3 = (bf16[2,512,12,64]{1,0,3,2:T(2,128)(2,1)}, bf16[2,512,12,64]{1,0,3,2:T(2,128)(2,1)S(1)}, u32[]{:S(2)}) copy-start(bf16[2,512,12,64]{1,0,3,2:T(2,128)(2,1)S(1)} %reshape.64) | copy-start | bytes 4718596
  116.6 8.5 %copy-start.8 = (f32[12,64,64]{2,1,0:T(8,128)S(1)}, f32[12,64,64]{2,1,0:T(8,128)}, u32[]{:S(2)}) copy-start(f32[12,64,64]{2,1,0:T(8,128)} %param.13) | copy-start | bytes 589828
  116.6 8.5 %copy-start.6 = (f32[2,12,64,64]{3,2,1,0:T(8,128)S(1)}, f32[2,12,64,64]{3,2,1,0:T(8,128)}, u32[]{:S(2)}) copy-start(f32[2,12,64,64]{3,2,1,0:T(8,128)} %get-tuple-element.11) | copy-start | bytes 1179652
  116.6 9.0 %copy-start.5 = (f32[2,12,64,512]{3,2,1,0:T(8,128)S(1)}, f32[2,12,64,512]{3,2,1,0:T(8,128)}, u32[]{:S(2)}) copy-start(f32[2,12,64,512]{3,2,1,0:T(8,128)} %fusion) | copy-start | bytes 9437188
  125.0 1.4 copy-start.4
  130.6 0.9 copy-start.9
  131.5 1.3 copy-start.10
  131.5 1.8 %copy-start.13 = (bf16[1024,768]{0,1:T(8,128)(2,1)S(1)}, bf16[1024,768]{0,1:T(8,128)(2,1)}, u32[]{:S(2)}) copy-start(bf16[1024,768]{0,1:T(8,128)(2,1)} %copy-done.12) | copy-start | bytes 4718596
  133.3 5.2 %copy-start.1 = (bf16[768,2304]{1,0:T(8,128)(2,1)S(1)}, bf16[768,2304]{1,0:T(8,128)(2,1)}, u32[]{:S(2)}) copy-start(bf16[768,2304]{1,0:T(8,128)(2,1)} %param.10) | copy-start | bytes 10616836
Sparse Core Ops, SparseCore 0:
  52.1 64.4 all-gather.2
where the time goes:
time: 146 us; the launch traced here: 145 us
  waiting for transfers between devices  52 us (36%)
  matrix products  42 us (29%)
  local copies, waits for them, and re-layouts  34.2 us (23%)
  between operations  13.7 us (9%)
  starting transfers between devices  2.48 us (2%)
    all_gather x1, waiting for transfers between devices, shards(): every_state = lax.all_gather(local_state[None], 'inner', axis=0, tiled=True)  52 us
    dot_general x1, matrix products, shards(): jnp.einsum('bhts,bshd->bthd', scores, values_all, preferred_element_type=...  10.5 us
    dot_general x1, matrix products, shards(): jnp.einsum('n,nhij->hij', lower_dev, every_state, precision=lax.Precision...  8.42 us
    dot_general x1, matrix products, shards(): jnp.dot(tick_rows, conv_weight[row_width:], preferred_element_type=jnp.fl...  5.66 us
    slice x2, local copies, waits for them, and re-layouts, shards(): earlier_rows = jnp.concatenate([last_row, tick_rows[:-1]], 0)  5.64 us
    dot_general x1, matrix products, shards(): jnp.dot(earlier_rows, weight_prev, preferred_element_type=jnp.float32)  4.97 us
    dot_general x1, matrix products, shards(): jnp.dot(normed, qkv_weight, preferred_element_type=jnp.float32)  4.36 us
    reshape x1, local copies, waits for them, and re-layouts, shards(): tick_rows = ticks.reshape(token_count, row_width)  4.17 us
  transfers between devices with their start and end apart: 2, of which 1 were waited for; matrix products, arithmetic and copies ran while one was open for 19% of the time, Pallas kernels for 0%

commit v1 on v0

--- a/solution.py
+++ b/solution.py
@@ -1,3 +1,4 @@
+import functools
 import jax
 import jax.numpy as jnp
 from jax import lax
@@ -5,6 +6,23 @@
 
 STRIDE = 8
 BLK = 512
+
+
+def scenes_recover(chunk, peer_axis, array_dim):
+    earlier, w1 = (lax.axis_size(peer_axis), lax.axis_index(peer_axis))
+    b_now, carry_out = (chunk, 1)
+    while carry_out < earlier:
+        block_last = lax.ppermute(
+            b_now, peer_axis, list(map(lambda w: (w, w ^ carry_out), range(earlier)))
+        )
+        b_next = jnp.concatenate([b_now, block_last], array_dim)
+        block_next = jnp.concatenate([block_last, b_now], array_dim)
+        b_now = jnp.where(w1 & carry_out == 0, b_next, block_next)
+        carry_out = 2 * carry_out
+    return b_now
+
+
+meet_ports = functools.partial(scenes_recover, peer_axis="inner", array_dim=0)
 
 
 def from_behind(value, axis, steps):
@@ -41,7 +59,7 @@
         "bthi,bthj->bhij", keys_all, values_all, preferred_element_type=jnp.float32
     )
     local_state = jnp.sum(block_states, 0)
-    every_state = lax.all_gather(local_state[None], "inner", axis=0, tiled=True)
+    every_state = meet_ports(local_state[None])
     lower_dev = (jnp.arange(every_state.shape[0]) < lax.axis_index("inner")).astype(jnp.float32)
     prefix = jnp.einsum("n,nhij->hij", lower_dev, every_state, precision=lax.Precision.HIGHEST)
     carried = state_in + prefix

time: 146 us -> 265 us (1.82)
  waiting for transfers between devices: 52 us -> 169 us
  between operations: 13.7 us -> 0.31 us
  other arithmetic: 1.04 us -> 10.8 us
  starting transfers between devices: 2.48 us -> 11 us
  matrix products: 42 us -> 38.4 us
    ppermute x0 -> x4, waiting for transfers between devices: none -> 169 us  [scenes_recover(): lax.ppermute(b_now, peer_axis, list(map(lambda w: (w, w ^ carry_out), ran...]
    all_gather x1 -> x0, waiting for transfers between devices: 52 us -> none  [shards(): every_state = lax.all_gather(local_state[None], 'inner', axis=0, tiled=True)]
    ppermute x0 -> x4, starting transfers between devices: none -> 8.54 us  [scenes_recover(): lax.ppermute(b_now, peer_axis, list(map(lambda w: (w, w ^ carry_out), ran...]
    select_n x0 -> x4, other arithmetic: none -> 7.87 us  [scenes_recover(): b_now = jnp.where(w1 & carry_out == 0, b_next, block_next)]
    reshape x1, local copies, waits for them, and re-layouts: 1.18 us -> 3.85 us  [shards(): qkv[:, :model_width].reshape(block_count, BLK, head_count, head_size)]
  transfers between devices with their start and end apart: 2 -> 5, of which waited for: 1 -> 4; matrix products, arithmetic and copies ran while one was open for 19% -> 13% of each run, Pallas kernels for 0% -> 0%
where the time goes in v1:
time: 265 us; the launch traced here: 264 us
  waiting for transfers between devices  169 us (64%)
  matrix products  38.4 us (14%)
  local copies, waits for them, and re-layouts  34.5 us (13%)
  starting transfers between devices  11 us (4%)
  other arithmetic  10.8 us (4%)
    ppermute x4, waiting for transfers between devices, scenes_recover(): lax.ppermute(b_now, peer_axis, list(map(lambda w: (w, w ^ carry_out), ran...  169 us
    dot_general x1, matrix products, shards(): jnp.einsum('bhts,bshd->bthd', scores, values_all, preferred_element_type=...  10.2 us
    ppermute x4, starting transfers between devices, scenes_recover(): lax.ppermute(b_now, peer_axis, list(map(lambda w: (w, w ^ carry_out), ran...  8.54 us
    select_n x4, other arithmetic, scenes_recover(): b_now = jnp.where(w1 & carry_out == 0, b_next, block_next)  7.87 us
    dot_general x1, matrix products, shards(): jnp.einsum('n,nhij->hij', lower_dev, every_state, precision=lax.Precision...  5.99 us
    slice x2, local copies, waits for them, and re-layouts, shards(): earlier_rows = jnp.concatenate([last_row, tick_rows[:-1]], 0)  5.66 us
    dot_general x1, matrix products, shards(): jnp.dot(tick_rows, conv_weight[row_width:], preferred_element_type=jnp.fl...  5.66 us
  transfers between devices with their start and end apart: 5, of which 4 were waited for; matrix products, arithmetic and copies ran while one was open for 13% of the time, Pallas kernels for 0%

profile of v1, /device:TPU:0, one launch (start us, length us, event | category | flops | bytes accessed | tf_op | source)
XLA Modules:
  0.0 264.4 jit_solution(6494431134777391270)
XLA Ops:
  0.8 2.5 collective-permute-start
  3.3 4.2 %reshape.62 = bf16[1024,1024]{1,0:T(8,128)(2,1)} reshape(bf16[8192,128]{1,0:T(8,128)(2,1)} %param.7) | data formatting | bytes 4194304 | tf_op jit(solution)/shard_map/reshape | solution.py:37
  7.5 5.7 %fusion.21 = f32[1024,768]{0,1:T(8,128)} fusion(bf16[1024,1024]{1,0:T(8,128)(2,1)} %reshape.62, bf16[2048,768]{1,0:T(8,128)(2,1)} %param.8), kind=kOutput, calls=%fused_computation.31 | convolution fusion | flops 1610612736 | bytes 6815744 | tf_op jit(solution)/shard_map/dot_general | solution.py:39
  13.2 1.5 slice.30
  14.7 4.2 %slice.31 = bf16[1023,1024]{1,0:T(8,128)(2,1)} reshape(bf16[8184,128]{1,0:T(8,128)(2,1)} %slice.30) | data formatting | bytes 4190208 | tf_op jit(solution)/shard_map/slice | solution.py:41
  18.8 5.0 %fusion.7 = (f32[1024]{0:T(1024)S(1)}, bf16[1024,768]{0,1:T(8,128)(2,1)S(1)}) fusion(f32[1024,768]{0,1:T(8,128)} %fusion.21, bf16[2048,768]{1,0:T(8,128)(2,1)} %param.8, bf16[1023,1024]{1,0:T(8,128)(2,1)} %slice.31, bf16[1,1024]{1,0:T(2,128)(2,1)S(1)} %collective-permute-done), kind=kOutput, calls=%fused_computation.12 | convolution fusion | flops 1618738176 | bytes 8394752 | tf_op jit(solution)/shard_map/dot_general | solution.py:42
  23.9 4.4 %convolution_convert_fusion = bf16[1024,2304]{1,0:T(8,128)(2,1)S(1)} fusion(bf16[768,2304]{1,0:T(8,128)(2,1)S(1)} %copy-done, bf16[1024,768]{0,1:T(8,128)(2,1)S(1)} %get-tuple-element.9, f32[768]{0:T(1024)S(1)} %copy-done.11, f32[1024]{0:T(1024)S(1)} %add_rsqrt_fusion.1), kind=kOutput, calls=%fused_computation.8 | convolution fusion | flops 3629383680 | bytes 9837568 | tf_op jit(solution)/shard_map/dot_general | solution.py:48
  28.2 1.5 fusion.44
  29.7 1.6 copy.41
  31.3 3.8 %reshape.65 = bf16[2,512,12,64]{1,0,3,2:T(2,128)(2,1)} reshape(bf16[1024,768]{0,1:T(8,128)(2,1)} %copy.41) | data formatting | bytes 3145728 | tf_op jit(solution)/shard_map/reshape | solution.py:54
  35.9 2.5 reshape.63
  38.4 2.9 %fusion.45 = (f32[12,64,64]{2,1,0:T(8,128)S(1)}, f32[2,12,64,64]{3,2,1,0:T(8,128)}) fusion(bf16[2,512,12,64]{1,0,3,2:T(2,128)(2,1)} %reshape.63, bf16[2,512,12,64]{1,0,3,2:T(2,128)(2,1)S(1)} %copy-done.7), kind=kOutput, calls=%fused_computation.57 | convolution fusion | flops 100712448 | bytes 3735552 | tf_op jit(solution)/shard_map/bthi,bthj->bhij/dot_general | solution.py:58
  41.3 2.6 collective-permute-start.1
  43.9 1.3 collective-permute-done.1
  45.3 1.6 collective-permute-start.2
  46.9 18.3 %collective-permute-done.2 = f32[2,12,64,64]{3,2,1,0:T(8,128)S(1)} collective-permute-done((f32[2,12,64,64]{3,2,1,0:T(8,128)S(1)}, f32[2,12,64,64]{3,2,1,0:T(8,128)S(1)}, u32[]{:S(2)}, u32[]{:S(2)}) %collective-permute-start.2) | collective-permute-done | bytes 393248 | tf_op jit(solution)/shard_map/ppermute | solution.py:15
  65.5 1.6 collective-permute-start.3
  67.1 34.4 %collective-permute-done.3 = f32[4,12,64,64]{3,2,1,0:T(8,128)} collective-permute-done((f32[4,12,64,64]{3,2,1,0:T(8,128)S(1)}, f32[4,12,64,64]{3,2,1,0:T(8,128)}, u32[]{:S(2)}, u32[]{:S(2)}) %collective-permute-start.3) | collective-permute-done | bytes 786464 | tf_op jit(solution)/shard_map/ppermute | solution.py:15
  101.5 3.9 %maximum_select_fusion.1 = f32[8,12,64,64]{3,2,1,0:T(8,128)S(1)} fusion(f32[4,12,64,64]{3,2,1,0:T(8,128)} %collective-permute-done.3, f32[4,12,64,64]{3,2,1,0:T(8,128)} %copy-done.3, pred[]{:T(512)S(6)} %eq.13), kind=kLoop, calls=%fused_computation.16 | loop fusion | flops 1179648 | bytes 3145729 | tf_op jit(solution)/shard_map/jit(_where)/select_n | solution.py:20
  105.4 2.7 %collective-permute-start.4 = (f32[8,12,64,64]{3,2,1,0:T(8,128)S(1)}, f32[8,12,64,64]{3,2,1,0:T(8,128)}, u32[]{:S(2)}, u32[]{:S(2)}) collective-permute-start(f32[8,12,64,64]{3,2,1,0:T(8,128)S(1)} %maximum_select_fusion.1), channel_id=1, source_target_pairs={{0,8},{1,9},{2,10},{3,11},{4,12},{5,13},{6,14},{7,15},{8,0},{9,1},... | collective-permute-start | bytes 4718600 | tf_op jit(solution)/shard_map/ppermute | solution.py:15
  108.2 2.6 copy.40
  110.8 3.9 %reshape.64 = bf16[2,512,12,64]{1,0,3,2:T(2,128)(2,1)} reshape(bf16[1024,768]{0,1:T(8,128)(2,1)} %copy.40) | data formatting | bytes 3145728 | tf_op jit(solution)/shard_map/reshape | solution.py:53
  114.6 2.4 reduce-window_subtract_fusion
  117.0 10.2 %fusion = f32[2,12,64,512]{3,2,1,0:T(8,128)} fusion(pred[512,512]{1,0:T(8,128)(4,1)S(1)} %iota_compare_fusion, bf16[2,512,12,64]{1,0,3,2:T(2,128)(2,1)} %reshape.63, bf16[2,512,12,64]{1,0,3,2:T(2,128)(2,1)} %reshape.65, bf16[2,512,12,64]{1,0,3,2:T(2,128)(2,1)} %reshape.64), kind=kOutput, calls=%fused_computation.1 | convolution fusion | flops 1623195648 | bytes 8126464 | tf_op jit(solution)/shard_map/bhts,bshd->bthd/dot_general | solution.py:71
  127.2 115.4 %collective-permute-done.4 = f32[8,12,64,64]{3,2,1,0:T(8,128)} collective-permute-done((f32[8,12,64,64]{3,2,1,0:T(8,128)S(1)}, f32[8,12,64,64]{3,2,1,0:T(8,128)}, u32[]{:S(2)}, u32[]{:S(2)}) %collective-permute-start.4) | collective-permute-done | bytes 1572896 | tf_op jit(solution)/shard_map/ppermute | solution.py:15
  242.6 3.6 %maximum_select_fusion = f32[16,12,64,64]{3,2,1,0:T(8,128)S(1)} fusion(f32[8,12,64,64]{3,2,1,0:T(8,128)} %collective-permute-done.4, f32[8,12,64,64]{3,2,1,0:T(8,128)S(1)} %maximum_select_fusion.1, pred[]{:T(512)S(6)} %eq.12), kind=kLoop, calls=%fused_computation.5 | loop fusion | flops 2359296 | bytes 6291457 | tf_op jit(solution)/shard_map/jit(_where)/select_n | solution.py:20
  246.2 6.0 %fusion.5 = f32[1,12,64,64]{3,0,2,1:T(1,128)S(1)} fusion(f32[16,12,64,64]{3,2,1,0:T(8,128)S(1)} %maximum_select_fusion, s32[]{:T(128)S(6)} %axis_index.16), kind=kOutput, calls=%fused_computation.6 | convolution fusion | flops 9437200 | bytes 3342340 | tf_op jit(solution)/shard_map/n,nhij->hij/dot_general | solution.py:64
  252.3 1.7 multiply_reduce_fusion
  254.2 2.4 copy.49
  257.8 0.9 copy-done.10
  259.1 2.6 fusion.10
  261.8 2.6 copy.52
  (42 shorter events, 3.8 us)
Async XLA Ops:
  0.0 23.8 %copy-start = (bf16[768,2304]{1,0:T(8,128)(2,1)S(1)}, bf16[768,2304]{1,0:T(8,128)(2,1)}, u32[]{:S(2)}) copy-start(bf16[768,2304]{1,0:T(8,128)(2,1)} %param.10) | copy-start | bytes 10616836
  0.8 18.0 %collective-permute-start = (bf16[1,1024]{1,0:T(2,128)(2,1)S(1)}, bf16[1,1024]{1,0:T(2,128)(2,1)S(1)}, u32[]{:S(2)}, u32[]{:S(2)}) collective-permute-start(bf16[1,1024]{1,0:T(2,128)(2,1)S(1)} %bitcast.53), channel_id=1, source_target_pairs={{0,1},{1,2},{2,3},{3,4},{4,5},{5,6},{6,7},{7,8},{8,9},{9,10},{10,1... | collective-permute-start | bytes 6152 | tf_op jit(solution)/shard_map/ppermute | solution.py:31
  7.5 5.7 %copy-start.2 = (bf16[8192,128]{1,0:T(8,128)(2,1)S(1)}, bf16[8192,128]{1,0:T(8,128)(2,1)}, u32[]{:S(2)}) copy-start(bf16[8192,128]{1,0:T(8,128)(2,1)} %param.7) | copy-start | bytes 6291460
  18.8 5.0 %copy-start.11 = (f32[768]{0:T(1024)S(1)}, f32[768]{0:T(1024)}, u32[]{:S(2)}) copy-start(f32[768]{0:T(1024)} %param.9) | copy-start | bytes 9220
  23.8 4.4 %copy-start.12 = (bf16[1024,768]{0,1:T(8,128)(2,1)}, bf16[1024,768]{0,1:T(8,128)(2,1)S(1)}, u32[]{:S(2)}) copy-start(bf16[1024,768]{0,1:T(8,128)(2,1)S(1)} %get-tuple-element.9) | copy-start | bytes 4718596
  35.9 2.5 copy-start.7
  41.3 4.0 %collective-permute-start.1 = (f32[1,12,64,64]{3,2,1,0:T(8,128)S(1)}, f32[1,12,64,64]{3,2,1,0:T(8,128)S(1)}, u32[]{:S(2)}, u32[]{:S(2)}) collective-permute-start(f32[1,12,64,64]{3,2,1,0:T(8,128)S(1)} %bitcast.48), channel_id=1, source_target_pairs={{0,1},{1,0},{2,3},{3,2},{4,5},{5,4},{6,7},{7,6},{8,9},{9,8},{10,11... | collective-permute-start | bytes 589832 | tf_op jit(solution)/shard_map/ppermute | solution.py:15
  45.3 19.9 %collective-permute-start.2 = (f32[2,12,64,64]{3,2,1,0:T(8,128)S(1)}, f32[2,12,64,64]{3,2,1,0:T(8,128)S(1)}, u32[]{:S(2)}, u32[]{:S(2)}) collective-permute-start(f32[2,12,64,64]{3,2,1,0:T(8,128)S(1)} %maximum_select_fusion.3), channel_id=1, source_target_pairs={{0,2},{1,3},{2,0},{3,1},{4,6},{5,7},{6,4},{7,5},{8,10},{9,11},{10,... | collective-permute-start | bytes 1179656 | tf_op jit(solution)/shard_map/ppermute | solution.py:15
  65.5 1.7 copy-start.3
  65.5 36.0 %collective-permute-start.3 = (f32[4,12,64,64]{3,2,1,0:T(8,128)S(1)}, f32[4,12,64,64]{3,2,1,0:T(8,128)}, u32[]{:S(2)}, u32[]{:S(2)}) collective-permute-start(f32[4,12,64,64]{3,2,1,0:T(8,128)S(1)} %maximum_select_fusion.2), channel_id=1, source_target_pairs={{0,4},{1,5},{2,6},{3,7},{4,0},{5,1},{6,2},{7,3},{8,12},{9,13},{10,... | collective-permute-start | bytes 2359304 | tf_op jit(solution)/shard_map/ppermute | solution.py:15
  105.4 137.1 %collective-permute-start.4 = (f32[8,12,64,64]{3,2,1,0:T(8,128)S(1)}, f32[8,12,64,64]{3,2,1,0:T(8,128)}, u32[]{:S(2)}, u32[]{:S(2)}) collective-permute-start(f32[8,12,64,64]{3,2,1,0:T(8,128)S(1)} %maximum_select_fusion.1), channel_id=1, source_target_pairs={{0,8},{1,9},{2,10},{3,11},{4,12},{5,13},{6,14},{7,15},{8,0},{9,1},... | collective-permute-start | bytes 4718600 | tf_op jit(solution)/shard_map/ppermute | solution.py:15
  246.2 6.0 %copy-start.8 = (f32[12,64,64]{2,1,0:T(8,128)S(1)}, f32[12,64,64]{2,1,0:T(8,128)}, u32[]{:S(2)}) copy-start(f32[12,64,64]{2,1,0:T(8,128)} %param.13) | copy-start | bytes 589828
  246.2 6.1 %copy-start.4 = (bf16[2,512,12,64]{1,0,3,2:T(2,128)(2,1)S(1)}, bf16[2,512,12,64]{1,0,3,2:T(2,128)(2,1)}, u32[]{:S(2)}) copy-start(bf16[2,512,12,64]{1,0,3,2:T(2,128)(2,1)} %reshape.64) | copy-start | bytes 4718596
  246.2 6.1 %copy-start.5 = (f32[2,12,64,512]{3,2,1,0:T(8,128)S(1)}, f32[2,12,64,512]{3,2,1,0:T(8,128)}, u32[]{:S(2)}) copy-start(f32[2,12,64,512]{3,2,1,0:T(8,128)} %fusion) | copy-start | bytes 9437188
  246.2 6.1 %copy-start.6 = (f32[2,12,64,64]{3,2,1,0:T(8,128)S(1)}, f32[2,12,64,64]{3,2,1,0:T(8,128)}, u32[]{:S(2)}) copy-start(f32[2,12,64,64]{3,2,1,0:T(8,128)} %reduce-window_subtract_fusion) | copy-start | bytes 1179652
  256.6 0.8 copy-start.9
  257.4 1.3 copy-start.10
  257.4 1.8 copy-start.13
  259.1 5.2 %copy-start.1 = (bf16[768,2304]{1,0:T(8,128)(2,1)S(1)}, bf16[768,2304]{1,0:T(8,128)(2,1)}, u32[]{:S(2)}) copy-start(bf16[768,2304]{1,0:T(8,128)(2,1)} %param.10) | copy-start | bytes 10616836
